TPU v7x, 256 devices: a whole 4x4x8 slice. The times are simulated.
256 devices in a mesh: px: 8 (over y, core), py: 32 (over z, x).
Axes of the slice: x: 4, y: 4, z: 8, core: 2. Of those that a mesh axis runs over, the one named last changes fastest.
Arguments:
- gamma: float32 [256, 256, 256], P('px', 'py'), may hold values from -10 to 10
- positions: float32 [3, 262144], P(None, ('px', 'py')), may hold values from 0 to 16
- weights: float32 [262144], P(('px', 'py')), may hold values from -4 to 4
- block_order: int32 [256, 1024], P(('px', 'py')), may hold values from 0 to 1023, each once within a row
- cell_index: int32 [262144], P(('px', 'py')), may hold values from 0 to 65535
- pair_dest: int32 [65536, 1], P(('px', 'py')), may hold values from 0 to 255; in each aligned block of 256 rows (0 to 255, 256 to 511, ...) at most 2 rows name the same one
- pair_blocks: int32 [2, 65536], P(None, ('px', 'py')), may hold values from 0 to 7
Outputs:
- stress: float32 [256, 256, 256], P('px', 'py')
- glide_force: float32 [262144], P(('px', 'py'))
- new_gamma: float32 [256, 256, 256], P('px', 'py')
Inputs may be any that keep to these rules, and one draw needn't show every extreme that they name: `pair_dest`: among the pairs of one device, at most 2 name the same destination device, a bound that some block reaches of them. `block_order`: each row is a permutation of the device's 1024 segments.
All inputs are finite; a program needn't handle non-finite values.
Results may differ from a plain program's by a relative error of at most 0.0003.
Values sent between devices are 32-bit elements; how exact they have to be, the bound alone decides.
No kernel may reach another device: no remote copies, remote signals or barrier semaphores. Data moves between devices by JAX's collectives and lax.ppermute only.
A program may use at most 64 MiB of HBM per device.

v0:
```python
import math

import jax
import jax.numpy as jnp
from jax import lax
from jax.experimental import pallas as pl
from jax.sharding import PartitionSpec as P

BLK = 128


POISSON = 0.34
STEP_MOBILITY = 0.5
CORE_SQUARED = 1.0
ROOT_HALF = 0.7071067811865476


def wrapped(indices, number):
    shifted = jnp.where(indices == number // 2, 0, indices - number)
    return jnp.where(indices < number // 2, indices, shifted).astype(jnp.float32)


def multiplier(first, second, third):
    summed = first * first + second * second + third * third
    bounded = jnp.maximum(summed, 1.0)
    normal_part = (first + second + third) ** 2 / (3.0 * bounded)
    slip_part = (first - second) ** 2 / (2.0 * bounded)
    factor = normal_part + slip_part - 2.0 * normal_part * slip_part / (1.0 - POISSON) - 1.0
    return jnp.where(summed > 0.5, factor, 0.0)


def pair_terms(target, source):
    offset = target[:, 0:3, :, None] - source[:, 0:3, None, :]
    squared = (
        offset[:, 0] * offset[:, 0]
        + offset[:, 1] * offset[:, 1]
        + offset[:, 2] * offset[:, 2]
        + CORE_SQUARED
    )
    along = (offset[:, 0] - offset[:, 1]) * ROOT_HALF
    strength = target[:, 3, :, None] * source[:, 3, None, :]
    coupling = strength * along / (squared * jnp.sqrt(squared))
    return (jnp.sum(coupling, axis=2), -jnp.sum(coupling, axis=1))


PAIR_STEP = 32


def pair_kernel(target_ref, source_ref, on_target_ref, on_source_ref):
    columns = jnp.transpose(target_ref[...].reshape(PAIR_STEP * 4, BLK))
    source_rows = []
    target_rows = []
    for p in range(PAIR_STEP):
        source = source_ref[p]
        d0 = columns[:, 4 * p : 4 * p + 1] - source[0:1, :]
        d1 = columns[:, 4 * p + 1 : 4 * p + 2] - source[1:2, :]
        d2 = columns[:, 4 * p + 2 : 4 * p + 3] - source[2:3, :]
        squared = d0 * d0 + d1 * d1 + d2 * d2 + CORE_SQUARED
        along = (d0 - d1) * ROOT_HALF
        strength = columns[:, 4 * p + 3 : 4 * p + 4] * source[3:4, :]
        root = lax.rsqrt(squared)
        coupling = strength * along * (root * root * root)
        source_rows.append(-jnp.sum(coupling, axis=0, keepdims=True))
        target_rows.append(jnp.sum(jnp.transpose(coupling), axis=0, keepdims=True))
    on_source_ref[...] = jnp.concatenate(source_rows, 0)
    on_target_ref[...] = jnp.concatenate(target_rows, 0)


def evaluate(target, source):
    number = target.shape[0]
    width = target.shape[2]
    block_in = pl.BlockSpec((PAIR_STEP, 4, width), lambda i: (i, 0, 0))
    block_out = pl.BlockSpec((PAIR_STEP, width), lambda i: (i, 0))
    return pl.pallas_call(
        pair_kernel,
        grid=(number // PAIR_STEP,),
        in_specs=[block_in, block_in],
        out_specs=[block_out, block_out],
        out_shape=[jax.ShapeDtypeStruct((number, width), jnp.float32)] * 2,
    )(target, source)


def dft_tables(number):
    indices = jnp.arange(number, dtype=jnp.int32)
    phases = indices[:, None] * indices[None, :] % number
    angles = phases.astype(jnp.float32) * (2.0 * math.pi / number)
    return (jnp.cos(angles), jnp.sin(angles))


def contract(form, left, right):
    return jnp.einsum(form, left, right, precision=lax.Precision.HIGHEST)


def rotate(form, real_part, imag_part, cosines, sine_table, direction):
    real_out = contract(form, real_part, cosines) + direction * contract(
        form, imag_part, sine_table
    )
    imag_out = contract(form, imag_part, cosines) - direction * contract(
        form, real_part, sine_table
    )
    return (real_out, imag_out)


def across_rows(real_part, imag_part):
    return (
        lax.all_to_all(real_part, "py", split_axis=1, concat_axis=2, tiled=True),
        lax.all_to_all(imag_part, "py", split_axis=1, concat_axis=2, tiled=True),
    )


def across_columns(real_part, imag_part):
    return (
        lax.all_to_all(real_part, "px", split_axis=0, concat_axis=2, tiled=True),
        lax.all_to_all(imag_part, "px", split_axis=0, concat_axis=2, tiled=True),
    )


def cplx_table(number, direction):
    cosines, sine_table = dft_tables(number)
    top = jnp.stack([cosines, -direction * sine_table], 1)
    bottom = jnp.stack([direction * sine_table, cosines], 1)
    return jnp.stack([top, bottom], 0)


def one_hot(indices, number):
    return (indices[:, None] == jnp.arange(number, dtype=jnp.int32)[None, :]).astype(jnp.float32)


def shards(gamma, positions, weights, block_order, cell_index, pair_dest, pair_blocks):
    extent = gamma.shape[2]
    py_count = extent // gamma.shape[1]
    half = extent // 2 + 1
    kept = -(-half // py_count) * py_count
    cosines, sine_table = dft_tables(extent)
    live = (jnp.arange(kept) < half).astype(jnp.float32)
    cos_half = cosines[:, :kept] * live[None, :]
    sin_half = sine_table[:, :kept] * live[None, :]
    folds = jnp.where((jnp.arange(kept) == 0) | (jnp.arange(kept) == extent // 2), 1.0, 2.0) * live
    forward = cplx_table(extent, 1.0)
    inverse = cplx_table(extent, -1.0)
    spec = contract("abx,xck->cakb", gamma, jnp.stack([cos_half, -sin_half], 1))
    spec = lax.all_to_all(spec, "py", split_axis=2, concat_axis=3, tiled=True)
    spec = contract("caky,cydm->dmka", spec, forward)
    spec = lax.all_to_all(spec, "px", split_axis=1, concat_axis=3, tiled=True)
    spec = contract("cmkz,czdq->dmkq", spec, forward)
    rows_local = spec.shape[1]
    cols_local = spec.shape[2]
    first_index = lax.axis_index("px") * rows_local + jnp.arange(rows_local, dtype=jnp.int32)
    second_index = lax.axis_index("py") * cols_local + jnp.arange(cols_local, dtype=jnp.int32)
    third_index = jnp.arange(extent, dtype=jnp.int32)
    factor_table = multiplier(
        wrapped(third_index, extent)[None, None, :],
        wrapped(first_index, extent)[:, None, None],
        wrapped(second_index, extent)[None, :, None],
    )
    spec = spec * factor_table[None]
    spec = contract("cmkq,cqdz->dzkm", spec, inverse)
    spec = lax.all_to_all(spec, "px", split_axis=1, concat_axis=3, tiled=True)
    spec = contract("cakm,cmdy->dayk", spec, inverse)
    spec = lax.all_to_all(spec, "py", split_axis=2, concat_axis=3, tiled=True)
    final_table = jnp.stack([folds[:, None] * cos_half.T, -folds[:, None] * sin_half.T], 0)
    stress = contract("cabk,ckx->abx", spec, final_table) / float(extent**3)
    seg_count = positions.shape[1]
    members = block_order[0]
    payload = jnp.concatenate([positions, weights[None, :]], 0)
    order_hot = one_hot(members, seg_count)
    blocks = jnp.transpose(
        contract("cs,ks->ck", payload, order_hot).reshape(4, -1, BLK), (1, 0, 2)
    )
    local_blocks = blocks.shape[0]
    seg_width = blocks.shape[2]
    flat_blocks = blocks.reshape(local_blocks, 4 * seg_width)
    source_local = pair_blocks[0]
    target_block = pair_blocks[1]
    destination = pair_dest[:, 0]
    pairs = destination.shape[0]
    devices = lax.psum(1, ("px", "py"))
    cap = 2
    earlier = jnp.sum(
        (destination[:, None] == destination[None, :])
        & (jnp.arange(pairs)[:, None] > jnp.arange(pairs)[None, :]),
        axis=1,
        dtype=jnp.int32,
    )
    slot = destination * cap + earlier
    slot_match = slot[:, None] == jnp.arange(devices * cap, dtype=jnp.int32)[None, :]
    wanted = jnp.sum(jnp.where(slot_match, target_block[:, None], 0), axis=0, dtype=jnp.int32)
    asked = lax.all_to_all(
        wanted.reshape(devices, cap), ("px", "py"), 0, 0, tiled=True
    ).reshape(-1)
    asked_hot = one_hot(asked, local_blocks)
    served = contract("pb,bw->pw", asked_hot, flat_blocks).reshape(devices, cap * 4 * seg_width)
    fetched = lax.all_to_all(served, ("px", "py"), 0, 0, tiled=True).reshape(
        devices * cap, 4 * seg_width
    )
    slot_hot = slot_match.astype(jnp.float32)
    source_hot = one_hot(source_local, local_blocks)
    target_rows = contract("ps,sw->pw", slot_hot, fetched).reshape(pairs, 4, seg_width)
    source_rows = contract("pb,bw->pw", source_hot, flat_blocks).reshape(pairs, 4, seg_width)
    on_target, on_source = evaluate(target_rows, source_rows)
    returned = contract("ps,pw->sw", slot_hot, on_target)
    arrived = lax.all_to_all(
        returned.reshape(devices, cap * seg_width), ("px", "py"), 0, 0, tiled=True
    ).reshape(devices * cap, seg_width)
    block_force = contract("pb,pw->bw", asked_hot, arrived) + contract(
        "pb,pw->bw", source_hot, on_source
    )
    pair_force = contract("k,ks->s", block_force.reshape(-1), order_hot)
    rows = gamma.shape[0] * gamma.shape[1]
    row_hot = one_hot(cell_index // extent, rows)
    column_hot = one_hot(cell_index % extent, extent)
    picked = contract("sr,rc->sc", row_hot, stress.reshape(rows, extent))
    glide_force = weights * jnp.sum(picked * column_hot, axis=1) + pair_force
    update = (STEP_MOBILITY * weights * glide_force)[:, None] * column_hot
    new_gamma = (gamma.reshape(rows, extent) + contract("sr,sc->rc", row_hot, update)).reshape(
        gamma.shape
    )
    return (stress, glide_force, new_gamma)


def solution(mesh):
    in_specs = (
        P("px", "py", None),
        P(None, ("px", "py")),
        P(("px", "py")),
        P(("px", "py"), None),
        P(("px", "py")),
        P(("px", "py"), None),
        P(None, ("px", "py")),
    )
    out_specs = (P("px", "py", None), P(("px", "py")), P("px", "py", None))
    return jax.shard_map(shards, mesh=mesh, in_specs=in_specs, out_specs=out_specs, check_vma=False)
```

profile of v0, /device:TPU:1, one launch (start us, length us, event | category | flops | bytes accessed | tf_op | source)
XLA Modules:
  0.0 210.5 jit_solution(3017429581862469036)
XLA Ops:
  5.7 11.9 %all-to-all-start = ((f32[32,1,2560]{2,1,0:T(1,128)}), f32[32,1,2560]{2,1,0:T(1,128)S(1)}, u32[]{:S(2)}, u32[]{:S(2)}) async-start(f32[32,1,2560]{2,1,0:T(1,128)} %reshape.347), calls=%async_computation | async-start | bytes 655360 | tf_op jit(solution)/shard_map/all_to_all | solution.py:142
  21.0 9.3 %all-to-all-done = f32[32,1,2560]{2,1,0:T(1,128)S(1)} async-done(((f32[32,1,2560]{2,1,0:T(1,128)}), f32[32,1,2560]{2,1,0:T(1,128)S(1)}, u32[]{:S(2)}, u32[]{:S(2)}) %all-to-all-start) | async-done | bytes 327712 | tf_op jit(solution)/shard_map/all_to_all | solution.py:142
  32.5 2.4 %fusion.8 = f32[2,256,5,32]{1,3,2,0:T(8,128)S(1)} fusion(f32[2,32,5,32,8]{1,4,0,2,3:T(8,128)S(1)} %bitcast.185, f32[1,256,2,256]{3,1,0,2:T(8,128)S(1)} %get-tuple-element.10, f32[1,256,2,256]{3,1,0,2:T(8,128)S(1)} %get-tuple-element.17), kind=kOutput, calls=%fused_computation.14 | convolution fusion | flops 503578624 | bytes 1703936 | tf_op jit(solution)/shard_map/caky,cydm->dmka/dot_general | solution.py:91
  35.9 2.0 reshape.349
  37.9 6.8 %all-to-all-start.1 = ((f32[8,1,10240]{2,1,0:T(1,128)}), f32[8,1,10240]{2,1,0:T(1,128)S(1)}, u32[]{:S(2)}, u32[]{:S(2)}) async-start(f32[8,1,10240]{2,1,0:T(1,128)} %reshape.349), calls=%async_computation.1 | async-start | bytes 655360 | tf_op jit(solution)/shard_map/all_to_all | solution.py:144
  46.3 5.4 %all-to-all-done.1 = f32[8,1,10240]{2,1,0:T(1,128)S(1)} async-done(((f32[8,1,10240]{2,1,0:T(1,128)}), f32[8,1,10240]{2,1,0:T(1,128)S(1)}, u32[]{:S(2)}, u32[]{:S(2)}) %all-to-all-start.1) | async-done | bytes 327712 | tf_op jit(solution)/shard_map/all_to_all | solution.py:144
  51.7 8.0 %all-to-all-start.4 = ((s32[256,1,2]{2,1,0:T(1,128)}), s32[256,1,2]{2,1,0:T(1,128)}, u32[]{:S(2)}, u32[]{:S(2)}) async-start(s32[256,1,2]{2,1,0:T(1,128)} %bitcast.53), calls=%async_computation.4 | async-start | bytes 262144 | tf_op jit(solution)/shard_map/all_to_all | solution.py:188
  64.3 1.8 fusion.12
  67.8 2.0 reshape.351
  69.8 1.8 all-to-all-done.4
  71.6 4.3 %all-to-all-start.2 = ((f32[8,1,10240]{2,1,0:T(1,128)}), f32[8,1,10240]{2,1,0:T(1,128)S(1)}, u32[]{:S(2)}, u32[]{:S(2)}) async-start(f32[8,1,10240]{2,1,0:T(1,128)} %reshape.351), calls=%async_computation.2 | async-start | bytes 655360 | tf_op jit(solution)/shard_map/all_to_all | solution.py:158
  75.9 2.0 fusion.15
  78.5 1.9 reduce.4
  81.1 2.3 %all_to_all.92 = f32[256,1,1024]{2,1,0:T(1,128)} reshape(f32[512,512]{1,0:T(8,128)S(1)} %fusion.51) | data formatting | bytes 2097152 | tf_op jit(solution)/shard_map/all_to_all | solution.py:193
  83.4 24.5 %all-to-all-start.5 = ((f32[256,1,1024]{2,1,0:T(1,128)}), f32[256,1,1024]{2,1,0:T(1,128)}, u32[]{:S(2)}, u32[]{:S(2)}) async-start(f32[256,1,1024]{2,1,0:T(1,128)} %all_to_all.92), calls=%async_computation.5 | async-start | bytes 2097152 | tf_op jit(solution)/shard_map/all_to_all | solution.py:193
  113.9 2.0 reshape.353
  115.9 22.1 %all-to-all-done.5 = f32[256,1,1024]{2,1,0:T(1,128)} async-done(((f32[256,1,1024]{2,1,0:T(1,128)}), f32[256,1,1024]{2,1,0:T(1,128)}, u32[]{:S(2)}, u32[]{:S(2)}) %all-to-all-start.5) | async-done | bytes 1048608 | tf_op jit(solution)/shard_map/all_to_all | solution.py:193
  138.0 3.9 %all-to-all-start.3 = ((f32[32,1,2560]{2,1,0:T(1,128)}), f32[32,1,2560]{2,1,0:T(1,128)S(1)}, u32[]{:S(2)}, u32[]{:S(2)}) async-start(f32[32,1,2560]{2,1,0:T(1,128)} %reshape.353), calls=%async_computation.3 | async-start | bytes 655360 | tf_op jit(solution)/shard_map/all_to_all | solution.py:160
  143.5 3.7 %reduce.1 = f32[256,1024]{1,0:T(8,128)S(1)} reduce(f32[256,1,1024]{2,1,0:T(1,128)} %all-to-all-done.5, f32[]{:T(128)} %constant.105), dimensions={1}, to_apply=%all_to_all.89.reduce_sub_computation | reduce | bytes 2097156 | tf_op jit(solution)/shard_map/all_to_all | solution.py:193
  149.6 26.8 %shard_map.94 = (f32[256,128]{1,0:T(8,128)}, f32[256,128]{1,0:T(8,128)}) custom-call(f32[256,4,128]{2,1,0:T(4,128)} %copy.101.target_ref, f32[256,4,128]{2,1,0:T(4,128)} %copy.102.source_ref), custom_call_target="tpu_custom_call" | custom-call | tf_op jit(solution)/shard_map/pallas_call | solution.py:74
  176.4 2.3 %fusion.28 = f32[512,128]{1,0:T(8,128)} fusion(f32[256,128]{1,0:T(8,128)} %get-tuple-element.5, s32[256]{0:T(256)S(1)} %bitcast.200), kind=kOutput, calls=%fused_computation.47 | convolution fusion | flops 201457664 | bytes 394240 | tf_op jit(solution)/shard_map/ps,pw->sw/dot_general | solution.py:91
  178.7 12.4 %all-to-all-start.6 = ((f32[256,1,256]{2,1,0:T(1,128)}), f32[256,1,256]{2,1,0:T(1,128)S(1)}, u32[]{:S(2)}, u32[]{:S(2)}) async-start(f32[256,1,256]{2,1,0:T(1,128)} %bitcast.66), calls=%async_computation.6 | async-start | bytes 524288 | tf_op jit(solution)/shard_map/all_to_all | solution.py:202
  196.4 9.4 %all-to-all-done.6 = f32[256,1,256]{2,1,0:T(1,128)S(1)} async-done(((f32[256,1,256]{2,1,0:T(1,128)}), f32[256,1,256]{2,1,0:T(1,128)S(1)}, u32[]{:S(2)}, u32[]{:S(2)}) %all-to-all-start.6) | async-done | bytes 262176 | tf_op jit(solution)/shard_map/all_to_all | solution.py:202
  208.5 1.7 fusion.14
  (96 shorter events, 38.3 us)
Async XLA Ops:
  4.3 14.3 %copy-start.11 = (s32[256,1]{0,1:T(1,128)S(1)}, s32[256,1]{0,1:T(1,128)}, u32[]{:S(2)}) copy-start(s32[256,1]{0,1:T(1,128)} %param.12) | copy-start | bytes 3076
  4.3 14.4 %copy-start.14 = (s32[2,256]{1,0:T(2,128)S(1)}, s32[2,256]{1,0:T(2,128)}, u32[]{:S(2)}) copy-start(s32[2,256]{1,0:T(2,128)} %param.13) | copy-start | bytes 6148
  5.7 24.6 %all-to-all-start = ((f32[32,1,2560]{2,1,0:T(1,128)}), f32[32,1,2560]{2,1,0:T(1,128)S(1)}, u32[]{:S(2)}, u32[]{:S(2)}) async-start(f32[32,1,2560]{2,1,0:T(1,128)} %reshape.347), calls=%async_computation | async-start | bytes 655360 | tf_op jit(solution)/shard_map/all_to_all | solution.py:142
  20.9 14.1 %copy-start.2 = (f32[1,256,2,256]{3,1,0,2:T(8,128)}, f32[1,256,2,256]{3,1,0,2:T(8,128)S(1)}, u32[]{:S(2)}) copy-start(f32[1,256,2,256]{3,1,0,2:T(8,128)S(1)} %get-tuple-element.10) | copy-start | bytes 1572868
  20.9 14.1 %copy-start.4 = (f32[1,256,2,256]{3,1,0,2:T(8,128)}, f32[1,256,2,256]{3,1,0,2:T(8,128)S(1)}, u32[]{:S(2)}) copy-start(f32[1,256,2,256]{3,1,0,2:T(8,128)S(1)} %get-tuple-element.17) | copy-start | bytes 1572868
  37.9 13.9 %all-to-all-start.1 = ((f32[8,1,10240]{2,1,0:T(1,128)}), f32[8,1,10240]{2,1,0:T(1,128)S(1)}, u32[]{:S(2)}, u32[]{:S(2)}) async-start(f32[8,1,10240]{2,1,0:T(1,128)} %reshape.349), calls=%async_computation.1 | async-start | bytes 655360 | tf_op jit(solution)/shard_map/all_to_all | solution.py:144
  51.7 19.9 %all-to-all-start.4 = ((s32[256,1,2]{2,1,0:T(1,128)}), s32[256,1,2]{2,1,0:T(1,128)}, u32[]{:S(2)}, u32[]{:S(2)}) async-start(s32[256,1,2]{2,1,0:T(1,128)} %bitcast.53), calls=%async_computation.4 | async-start | bytes 262144 | tf_op jit(solution)/shard_map/all_to_all | solution.py:188
  63.1 1.0 copy-start.3
  63.1 1.2 copy-start.5
  64.3 1.8 copy-start
  67.8 8.2 %copy-start.13 = (f32[1024]{0:T(1024)S(1)}, f32[1024]{0:T(1024)}, u32[]{:S(2)}) copy-start(f32[1024]{0:T(1024)} %param.9) | copy-start | bytes 12292
  67.8 8.2 %copy-start.15 = (f32[3,1024]{1,0:T(4,128)S(1)}, f32[3,1024]{1,0:T(4,128)}, u32[]{:S(2)}) copy-start(f32[3,1024]{1,0:T(4,128)} %param.8) | copy-start | bytes 36868
  67.8 8.1 %copy-start.16 = (s32[1,1024]{1,0:T(1,128)S(1)}, s32[1,1024]{1,0:T(1,128)}, u32[]{:S(2)}) copy-start(s32[1,1024]{1,0:T(1,128)} %param.10) | copy-start | bytes 12292
  71.6 11.8 %all-to-all-start.2 = ((f32[8,1,10240]{2,1,0:T(1,128)}), f32[8,1,10240]{2,1,0:T(1,128)S(1)}, u32[]{:S(2)}, u32[]{:S(2)}) async-start(f32[8,1,10240]{2,1,0:T(1,128)} %reshape.351), calls=%async_computation.2 | async-start | bytes 655360 | tf_op jit(solution)/shard_map/all_to_all | solution.py:158
  83.4 54.6 %all-to-all-start.5 = ((f32[256,1,1024]{2,1,0:T(1,128)}), f32[256,1,1024]{2,1,0:T(1,128)}, u32[]{:S(2)}, u32[]{:S(2)}) async-start(f32[256,1,1024]{2,1,0:T(1,128)} %all_to_all.92), calls=%async_computation.5 | async-start | bytes 2097152 | tf_op jit(solution)/shard_map/all_to_all | solution.py:193
  111.2 1.0 copy-start.1
  138.0 40.7 %all-to-all-start.3 = ((f32[32,1,2560]{2,1,0:T(1,128)}), f32[32,1,2560]{2,1,0:T(1,128)S(1)}, u32[]{:S(2)}, u32[]{:S(2)}) async-start(f32[32,1,2560]{2,1,0:T(1,128)} %reshape.353), calls=%async_computation.3 | async-start | bytes 655360 | tf_op jit(solution)/shard_map/all_to_all | solution.py:160
  148.4 42.6 %copy-start.12 = (s32[1024]{0:T(1024)S(1)}, s32[1024]{0:T(1024)}, u32[]{:S(2)}) copy-start(s32[1024]{0:T(1024)} %param.11) | copy-start | bytes 12292
  178.7 27.1 %all-to-all-start.6 = ((f32[256,1,256]{2,1,0:T(1,128)}), f32[256,1,256]{2,1,0:T(1,128)S(1)}, u32[]{:S(2)}, u32[]{:S(2)}) async-start(f32[256,1,256]{2,1,0:T(1,128)} %bitcast.66), calls=%async_computation.6 | async-start | bytes 524288 | tf_op jit(solution)/shard_map/all_to_all | solution.py:202
  193.8 0.9 copy-start.6
  193.8 1.0 copy-start.7
  194.8 11.4 %copy-start.10 = (f32[256,128]{1,0:T(8,128)S(1)}, f32[256,128]{1,0:T(8,128)}, u32[]{:S(2)}) copy-start(f32[256,128]{1,0:T(8,128)} %get-tuple-element.6) | copy-start | bytes 393220
  195.5 12.4 %copy-start.9 = (f32[32,8,256]{2,1,0:T(8,128)}, f32[32,8,256]{2,1,0:T(8,128)S(1)}, u32[]{:S(2)}) copy-start(f32[32,8,256]{2,1,0:T(8,128)S(1)} %fusion.13) | copy-start | bytes 786436
  195.5 13.0 %copy-start.8 = (f32[32,8,256]{2,1,0:T(8,128)S(1)}, f32[32,8,256]{2,1,0:T(8,128)}, u32[]{:S(2)}) copy-start(f32[32,8,256]{2,1,0:T(8,128)} %param.7) | copy-start | bytes 786436
where the time goes:
time: 214 us; the launch traced here: 210 us
  starting transfers between devices  71.7 us (34%)
  waiting for transfers between devices  48 us (22%)
  Pallas kernels  26.8 us (13%)
  local copies, waits for them, and re-layouts  26.1 us (12%)
  matrix products  18.8 us (9%)
  other arithmetic  17.6 us (8%)
    pallas_call x1, Pallas kernels, evaluate(): pl.pallas_call(pair_kernel, grid=(number // PAIR_STEP,), in_specs=[block_...  26.8 us
    all_to_all x1, starting transfers between devices, shards(): lax.all_to_all(served, ('px', 'py'), 0, 0, tiled=True)  24.5 us
    all_to_all x1, waiting for transfers between devices, shards(): lax.all_to_all(served, ('px', 'py'), 0, 0, tiled=True)  22.1 us
    dot_general x16, matrix products, contract(): return jnp.einsum(form, left, right, precision=lax.Precision.HIGHEST)  18.8 us
    all_to_all x2, starting transfers between devices, shards(): spec = lax.all_to_all(spec, 'py', split_axis=2, concat_axis=3, tiled=True)  15.7 us
    unnamed x42, local copies, waits for them, and re-layouts  12.8 us
    all_to_all x1, starting transfers between devices, shards(): lax.all_to_all(returned.reshape(devices, cap * seg_width), ('px', 'py'),...  12.4 us
    all_to_all x2, starting transfers between devices, shards(): spec = lax.all_to_all(spec, 'px', split_axis=1, concat_axis=3, tiled=True)  11.1 us
  transfers between devices with their start and end apart: 7, of which 5 were waited for; matrix products, arithmetic and copies ran while one was open for 19% of the time, Pallas kernels for 13%

commit v1 on v0

--- a/solution.py
+++ b/solution.py
@@ -61,7 +61,14 @@
         root = lax.rsqrt(squared)
         coupling = strength * along * (root * root * root)
         source_rows.append(-jnp.sum(coupling, axis=0, keepdims=True))
-        target_rows.append(jnp.sum(jnp.transpose(coupling), axis=0, keepdims=True))
+        high = coupling.astype(jnp.bfloat16)
+        low = (coupling - high.astype(jnp.float32)).astype(jnp.bfloat16)
+        ones = jnp.ones((8, BLK), jnp.bfloat16)
+        lanes = (((1,), (1,)), ((), ()))
+        sums = lax.dot_general(
+            ones, high, lanes, preferred_element_type=jnp.float32
+        ) + lax.dot_general(ones, low, lanes, preferred_element_type=jnp.float32)
+        target_rows.append(sums[0:1, :])
     on_source_ref[...] = jnp.concatenate(source_rows, 0)
     on_target_ref[...] = jnp.concatenate(target_rows, 0)
 

time: 214 us -> 211 us (0.986)
  Pallas kernels: 26.8 us -> 23.6 us
    pallas_call x1, Pallas kernels: 26.8 us -> 23.6 us  [evaluate(): pl.pallas_call(pair_kernel, grid=(number // PAIR_STEP,), in_specs=[block_...]
  transfers between devices with their start and end apart: 7 -> 7, of which waited for: 5 -> 5; matrix products, arithmetic and copies ran while one was open for 19% -> 19% of each run, Pallas kernels for 13% -> 11%
where the time goes in v1:
time: 211 us; the launch traced here: 207 us
  starting transfers between devices  71.5 us (34%)
  waiting for transfers between devices  48 us (23%)
  local copies, waits for them, and re-layouts  26.1 us (12%)
  Pallas kernels  23.6 us (11%)
  matrix products  18.8 us (9%)
  other arithmetic  17.6 us (8%)
    all_to_all x1, starting transfers between devices, shards(): lax.all_to_all(served, ('px', 'py'), 0, 0, tiled=True)  24.3 us
    pallas_call x1, Pallas kernels, evaluate(): pl.pallas_call(pair_kernel, grid=(number // PAIR_STEP,), in_specs=[block_...  23.6 us
    all_to_all x1, waiting for transfers between devices, shards(): lax.all_to_all(served, ('px', 'py'), 0, 0, tiled=True)  22.1 us
    dot_general x16, matrix products, contract(): return jnp.einsum(form, left, right, precision=lax.Precision.HIGHEST)  18.8 us
    all_to_all x2, starting transfers between devices, shards(): spec = lax.all_to_all(spec, 'py', split_axis=2, concat_axis=3, tiled=True)  15.7 us
    unnamed x42, local copies, waits for them, and re-layouts  12.8 us
    all_to_all x1, starting transfers between devices, shards(): lax.all_to_all(returned.reshape(devices, cap * seg_width), ('px', 'py'),...  12.4 us
    all_to_all x2, starting transfers between devices, shards(): spec = lax.all_to_all(spec, 'px', split_axis=1, concat_axis=3, tiled=True)  11.1 us
  transfers between devices with their start and end apart: 7, of which 5 were waited for; matrix products, arithmetic and copies ran while one was open for 19% of the time, Pallas kernels for 11%

profile of v1, /device:TPU:1, one launch (start us, length us, event | category | flops | bytes accessed | tf_op | source)
XLA Modules:
  0.0 207.1 jit_solution(8687408588260666082)
XLA Ops:
  5.7 11.9 %all-to-all-start = ((f32[32,1,2560]{2,1,0:T(1,128)}), f32[32,1,2560]{2,1,0:T(1,128)S(1)}, u32[]{:S(2)}, u32[]{:S(2)}) async-start(f32[32,1,2560]{2,1,0:T(1,128)} %reshape.347), calls=%async_computation | async-start | bytes 655360 | tf_op jit(solution)/shard_map/all_to_all | solution.py:149
  21.0 9.3 %all-to-all-done = f32[32,1,2560]{2,1,0:T(1,128)S(1)} async-done(((f32[32,1,2560]{2,1,0:T(1,128)}), f32[32,1,2560]{2,1,0:T(1,128)S(1)}, u32[]{:S(2)}, u32[]{:S(2)}) %all-to-all-start) | async-done | bytes 327712 | tf_op jit(solution)/shard_map/all_to_all | solution.py:149
  32.5 2.4 %fusion.8 = f32[2,256,5,32]{1,3,2,0:T(8,128)S(1)} fusion(f32[2,32,5,32,8]{1,4,0,2,3:T(8,128)S(1)} %bitcast.185, f32[1,256,2,256]{3,1,0,2:T(8,128)S(1)} %get-tuple-element.10, f32[1,256,2,256]{3,1,0,2:T(8,128)S(1)} %get-tuple-element.17), kind=kOutput, calls=%fused_computation.14 | convolution fusion | flops 503578624 | bytes 1703936 | tf_op jit(solution)/shard_map/caky,cydm->dmka/dot_general | solution.py:98
  35.9 2.0 reshape.349
  37.9 6.8 %all-to-all-start.1 = ((f32[8,1,10240]{2,1,0:T(1,128)}), f32[8,1,10240]{2,1,0:T(1,128)S(1)}, u32[]{:S(2)}, u32[]{:S(2)}) async-start(f32[8,1,10240]{2,1,0:T(1,128)} %reshape.349), calls=%async_computation.1 | async-start | bytes 655360 | tf_op jit(solution)/shard_map/all_to_all | solution.py:151
  46.3 5.4 %all-to-all-done.1 = f32[8,1,10240]{2,1,0:T(1,128)S(1)} async-done(((f32[8,1,10240]{2,1,0:T(1,128)}), f32[8,1,10240]{2,1,0:T(1,128)S(1)}, u32[]{:S(2)}, u32[]{:S(2)}) %all-to-all-start.1) | async-done | bytes 327712 | tf_op jit(solution)/shard_map/all_to_all | solution.py:151
  51.7 8.0 %all-to-all-start.4 = ((s32[256,1,2]{2,1,0:T(1,128)}), s32[256,1,2]{2,1,0:T(1,128)}, u32[]{:S(2)}, u32[]{:S(2)}) async-start(s32[256,1,2]{2,1,0:T(1,128)} %bitcast.53), calls=%async_computation.4 | async-start | bytes 262144 | tf_op jit(solution)/shard_map/all_to_all | solution.py:195
  64.3 1.8 fusion.12
  67.8 2.0 reshape.351
  69.8 1.8 all-to-all-done.4
  71.6 4.3 %all-to-all-start.2 = ((f32[8,1,10240]{2,1,0:T(1,128)}), f32[8,1,10240]{2,1,0:T(1,128)S(1)}, u32[]{:S(2)}, u32[]{:S(2)}) async-start(f32[8,1,10240]{2,1,0:T(1,128)} %reshape.351), calls=%async_computation.2 | async-start | bytes 655360 | tf_op jit(solution)/shard_map/all_to_all | solution.py:165
  75.9 2.0 fusion.15
  78.5 1.9 reduce.4
  81.1 2.3 %all_to_all.92 = f32[256,1,1024]{2,1,0:T(1,128)} reshape(f32[512,512]{1,0:T(8,128)S(1)} %fusion.51) | data formatting | bytes 2097152 | tf_op jit(solution)/shard_map/all_to_all | solution.py:200
  83.4 24.3 %all-to-all-start.5 = ((f32[256,1,1024]{2,1,0:T(1,128)}), f32[256,1,1024]{2,1,0:T(1,128)}, u32[]{:S(2)}, u32[]{:S(2)}) async-start(f32[256,1,1024]{2,1,0:T(1,128)} %all_to_all.92), calls=%async_computation.5 | async-start | bytes 2097152 | tf_op jit(solution)/shard_map/all_to_all | solution.py:200
  113.6 2.0 reshape.353
  115.7 22.1 %all-to-all-done.5 = f32[256,1,1024]{2,1,0:T(1,128)} async-done(((f32[256,1,1024]{2,1,0:T(1,128)}), f32[256,1,1024]{2,1,0:T(1,128)}, u32[]{:S(2)}, u32[]{:S(2)}) %all-to-all-start.5) | async-done | bytes 1048608 | tf_op jit(solution)/shard_map/all_to_all | solution.py:200
  137.8 3.9 %all-to-all-start.3 = ((f32[32,1,2560]{2,1,0:T(1,128)}), f32[32,1,2560]{2,1,0:T(1,128)S(1)}, u32[]{:S(2)}, u32[]{:S(2)}) async-start(f32[32,1,2560]{2,1,0:T(1,128)} %reshape.353), calls=%async_computation.3 | async-start | bytes 655360 | tf_op jit(solution)/shard_map/all_to_all | solution.py:167
  143.2 3.7 %reduce.1 = f32[256,1024]{1,0:T(8,128)S(1)} reduce(f32[256,1,1024]{2,1,0:T(1,128)} %all-to-all-done.5, f32[]{:T(128)} %constant.105), dimensions={1}, to_apply=%all_to_all.89.reduce_sub_computation | reduce | bytes 2097156 | tf_op jit(solution)/shard_map/all_to_all | solution.py:200
  149.3 23.6 %shard_map.94 = (f32[256,128]{1,0:T(8,128)}, f32[256,128]{1,0:T(8,128)}) custom-call(f32[256,4,128]{2,1,0:T(4,128)} %copy.101.target_ref, f32[256,4,128]{2,1,0:T(4,128)} %copy.102.source_ref), custom_call_target="tpu_custom_call" | custom-call | tf_op jit(solution)/shard_map/pallas_call | solution.py:81
  173.0 2.3 %fusion.28 = f32[512,128]{1,0:T(8,128)} fusion(f32[256,128]{1,0:T(8,128)} %get-tuple-element.5, s32[256]{0:T(256)S(1)} %bitcast.200), kind=kOutput, calls=%fused_computation.47 | convolution fusion | flops 201457664 | bytes 394240 | tf_op jit(solution)/shard_map/ps,pw->sw/dot_general | solution.py:98
  175.3 12.4 %all-to-all-start.6 = ((f32[256,1,256]{2,1,0:T(1,128)}), f32[256,1,256]{2,1,0:T(1,128)S(1)}, u32[]{:S(2)}, u32[]{:S(2)}) async-start(f32[256,1,256]{2,1,0:T(1,128)} %bitcast.66), calls=%async_computation.6 | async-start | bytes 524288 | tf_op jit(solution)/shard_map/all_to_all | solution.py:209
  193.0 9.4 %all-to-all-done.6 = f32[256,1,256]{2,1,0:T(1,128)S(1)} async-done(((f32[256,1,256]{2,1,0:T(1,128)}), f32[256,1,256]{2,1,0:T(1,128)S(1)}, u32[]{:S(2)}, u32[]{:S(2)}) %all-to-all-start.6) | async-done | bytes 262176 | tf_op jit(solution)/shard_map/all_to_all | solution.py:209
  205.1 1.7 fusion.14
  (96 shorter events, 38.3 us)
Async XLA Ops:
  4.3 14.3 %copy-start.11 = (s32[256,1]{0,1:T(1,128)S(1)}, s32[256,1]{0,1:T(1,128)}, u32[]{:S(2)}) copy-start(s32[256,1]{0,1:T(1,128)} %param.12) | copy-start | bytes 3076
  4.3 14.4 %copy-start.14 = (s32[2,256]{1,0:T(2,128)S(1)}, s32[2,256]{1,0:T(2,128)}, u32[]{:S(2)}) copy-start(s32[2,256]{1,0:T(2,128)} %param.13) | copy-start | bytes 6148
  5.7 24.6 %all-to-all-start = ((f32[32,1,2560]{2,1,0:T(1,128)}), f32[32,1,2560]{2,1,0:T(1,128)S(1)}, u32[]{:S(2)}, u32[]{:S(2)}) async-start(f32[32,1,2560]{2,1,0:T(1,128)} %reshape.347), calls=%async_computation | async-start | bytes 655360 | tf_op jit(solution)/shard_map/all_to_all | solution.py:149
  20.9 14.1 %copy-start.2 = (f32[1,256,2,256]{3,1,0,2:T(8,128)}, f32[1,256,2,256]{3,1,0,2:T(8,128)S(1)}, u32[]{:S(2)}) copy-start(f32[1,256,2,256]{3,1,0,2:T(8,128)S(1)} %get-tuple-element.10) | copy-start | bytes 1572868
  20.9 14.1 %copy-start.4 = (f32[1,256,2,256]{3,1,0,2:T(8,128)}, f32[1,256,2,256]{3,1,0,2:T(8,128)S(1)}, u32[]{:S(2)}) copy-start(f32[1,256,2,256]{3,1,0,2:T(8,128)S(1)} %get-tuple-element.17) | copy-start | bytes 1572868
  37.9 13.9 %all-to-all-start.1 = ((f32[8,1,10240]{2,1,0:T(1,128)}), f32[8,1,10240]{2,1,0:T(1,128)S(1)}, u32[]{:S(2)}, u32[]{:S(2)}) async-start(f32[8,1,10240]{2,1,0:T(1,128)} %reshape.349), calls=%async_computation.1 | async-start | bytes 655360 | tf_op jit(solution)/shard_map/all_to_all | solution.py:151
  51.7 19.9 %all-to-all-start.4 = ((s32[256,1,2]{2,1,0:T(1,128)}), s32[256,1,2]{2,1,0:T(1,128)}, u32[]{:S(2)}, u32[]{:S(2)}) async-start(s32[256,1,2]{2,1,0:T(1,128)} %bitcast.53), calls=%async_computation.4 | async-start | bytes 262144 | tf_op jit(solution)/shard_map/all_to_all | solution.py:195
  63.1 1.0 copy-start.3
  63.1 1.2 copy-start.5
  64.3 1.8 copy-start
  67.8 8.2 %copy-start.13 = (f32[1024]{0:T(1024)S(1)}, f32[1024]{0:T(1024)}, u32[]{:S(2)}) copy-start(f32[1024]{0:T(1024)} %param.9) | copy-start | bytes 12292
  67.8 8.2 %copy-start.15 = (f32[3,1024]{1,0:T(4,128)S(1)}, f32[3,1024]{1,0:T(4,128)}, u32[]{:S(2)}) copy-start(f32[3,1024]{1,0:T(4,128)} %param.8) | copy-start | bytes 36868
  67.8 8.1 %copy-start.16 = (s32[1,1024]{1,0:T(1,128)S(1)}, s32[1,1024]{1,0:T(1,128)}, u32[]{:S(2)}) copy-start(s32[1,1024]{1,0:T(1,128)} %param.10) | copy-start | bytes 12292
  71.6 11.8 %all-to-all-start.2 = ((f32[8,1,10240]{2,1,0:T(1,128)}), f32[8,1,10240]{2,1,0:T(1,128)S(1)}, u32[]{:S(2)}, u32[]{:S(2)}) async-start(f32[8,1,10240]{2,1,0:T(1,128)} %reshape.351), calls=%async_computation.2 | async-start | bytes 655360 | tf_op jit(solution)/shard_map/all_to_all | solution.py:165
  83.4 54.4 %all-to-all-start.5 = ((f32[256,1,1024]{2,1,0:T(1,128)}), f32[256,1,1024]{2,1,0:T(1,128)}, u32[]{:S(2)}, u32[]{:S(2)}) async-start(f32[256,1,1024]{2,1,0:T(1,128)} %all_to_all.92), calls=%async_computation.5 | async-start | bytes 2097152 | tf_op jit(solution)/shard_map/all_to_all | solution.py:200
  111.0 1.0 copy-start.1
  137.8 37.5 %all-to-all-start.3 = ((f32[32,1,2560]{2,1,0:T(1,128)}), f32[32,1,2560]{2,1,0:T(1,128)S(1)}, u32[]{:S(2)}, u32[]{:S(2)}) async-start(f32[32,1,2560]{2,1,0:T(1,128)} %reshape.353), calls=%async_computation.3 | async-start | bytes 655360 | tf_op jit(solution)/shard_map/all_to_all | solution.py:167
  148.2 39.5 %copy-start.12 = (s32[1024]{0:T(1024)S(1)}, s32[1024]{0:T(1024)}, u32[]{:S(2)}) copy-start(s32[1024]{0:T(1024)} %param.11) | copy-start | bytes 12292
  175.3 27.1 %all-to-all-start.6 = ((f32[256,1,256]{2,1,0:T(1,128)}), f32[256,1,256]{2,1,0:T(1,128)S(1)}, u32[]{:S(2)}, u32[]{:S(2)}) async-start(f32[256,1,256]{2,1,0:T(1,128)} %bitcast.66), calls=%async_computation.6 | async-start | bytes 524288 | tf_op jit(solution)/shard_map/all_to_all | solution.py:209
  190.4 0.9 copy-start.6
  190.4 1.0 copy-start.7
  191.4 11.4 %copy-start.10 = (f32[256,128]{1,0:T(8,128)S(1)}, f32[256,128]{1,0:T(8,128)}, u32[]{:S(2)}) copy-start(f32[256,128]{1,0:T(8,128)} %get-tuple-element.6) | copy-start | bytes 393220
  192.1 12.4 %copy-start.9 = (f32[32,8,256]{2,1,0:T(8,128)}, f32[32,8,256]{2,1,0:T(8,128)S(1)}, u32[]{:S(2)}) copy-start(f32[32,8,256]{2,1,0:T(8,128)S(1)} %fusion.13) | copy-start | bytes 786436
  192.1 13.0 %copy-start.8 = (f32[32,8,256]{2,1,0:T(8,128)S(1)}, f32[32,8,256]{2,1,0:T(8,128)}, u32[]{:S(2)}) copy-start(f32[32,8,256]{2,1,0:T(8,128)} %param.7) | copy-start | bytes 786436
